TPU v7x, 256 devices: a whole 4x4x8 slice. The times are simulated.
256 devices in a mesh: dp: 32 (over x, y, z_lo), tensor: 8 (over z_hi, core).
Axes of the slice: x: 4, y: 4, z: 8 (z_hi: 4, z_lo: 2; z = z_hi * 2 + z_lo), core: 2. Of those that a mesh axis runs over, the one named last changes fastest.
Arguments:
- arrivals: bfloat16 [32768, 2048], P('dp', 'tensor')
- deal: int32 [32, 32], P('dp'), may hold values from 0 to 1023, as said below
- seg_ids: int32 [32, 1024], P('dp'), may hold values from 0 to 7, never falling along the last dimension, each value on 1 to 512 neighbouring positions
- page_table: int32 [32, 8], P('dp'), may hold values from 0 to 7, each once within a row
- attn_gain: float32 [2048], replicated, may hold values from 0.1 to 1.9
- w_query: bfloat16 [2048, 1024], P(None, 'tensor'), may hold values from -0.125 to 0.125
- w_keyval: bfloat16 [2048, 512], replicated, may hold values from -0.125 to 0.125
- query_gain: float32 [64], replicated, may hold values from 0.1 to 1.9
- key_gain: float32 [64], replicated, may hold values from 0.1 to 1.9
- w_out: bfloat16 [1024, 2048], P('tensor'), may hold values from -0.1875 to 0.1875
- ffn_gain: float32 [2048], replicated, may hold values from 0.1 to 1.9
- w_gate: bfloat16 [2048, 5120], P(None, 'tensor'), may hold values from -0.125 to 0.125
- w_up: bfloat16 [2048, 5120], P(None, 'tensor'), may hold values from -0.125 to 0.125
- w_down: bfloat16 [5120, 2048], P('tensor'), may hold values from -0.078125 to 0.078125
Outputs:
- result: bfloat16 [32768, 2048], P('dp', 'tensor')
- kv_pages: bfloat16 [256, 128, 512], P('dp', None, 'tensor')
Inputs may be any that keep to these rules, and one draw needn't show every extreme that they name: deal[s, k] = g * 32 + j sends unit k of arrival block s to unit j of group g; every value occurs once; the units of one arrival block go to exactly 16 groups, 2 units to each. `seg_ids`: each row never falls; one prompt is one run of equal numbers. `page_table`: each row holds every page number once.
All inputs are finite; a program needn't handle non-finite values.
Results may differ from a plain program's by a relative error of at most 0.019.
Values may be sent and summed in bfloat16 or wider, within the bound.
No kernel may reach another device: no remote copies, remote signals or barrier semaphores. Data moves between devices by JAX's collectives and lax.ppermute only.
A program may use at most 128 MiB of HBM per device.

v0:
```python
import math
import jax
import jax.numpy as jnp
from jax import lax
from jax.sharding import PartitionSpec as P

HEAD = 64
KVH = 4
MOST = 2
PAGE = 128
EPS = 1e-06
THETA = 10000.0
BLOCK_ROWS = 512


def rms_scale(values, gain):
    values = values.astype(jnp.float32)
    mean_sq = jnp.mean(values * values, axis=-1, keepdims=True)
    return values * lax.rsqrt(mean_sq + EPS) * gain


def rope_tables(positions, width):
    half = width // 2
    inverse = THETA ** (-jnp.arange(half, dtype=jnp.float32) * 2.0 / width)
    angles = positions.astype(jnp.float32)[:, None] * inverse[None, :]
    return (jnp.cos(angles), jnp.sin(angles))


def rotate(values, cosine, sine):
    half = values.shape[-1] // 2
    first = values[..., :half]
    second = values[..., half:]
    cos_b = cosine[:, None, :]
    sin_b = sine[:, None, :]
    return jnp.concatenate(
        [first * cos_b - second * sin_b, second * cos_b + first * sin_b], axis=-1
    )


def segment_starts(seg_row):
    count = seg_row.shape[0]
    index = jnp.arange(count, dtype=jnp.int32)
    prior = jnp.concatenate([seg_row[:1] - 1, seg_row[:-1]])
    marks = jnp.where(seg_row != prior, index, 0)
    return lax.cummax(marks, axis=0)


def on_device(
    arrivals,
    deal,
    seg_ids,
    page_table,
    attn_gain,
    w_query,
    w_keyval,
    query_gain,
    key_gain,
    w_out,
    ffn_gain,
    w_gate,
    w_up,
    w_down,
):
    groups = lax.axis_size("dp")
    shards = lax.axis_size("tensor")
    tensor_rank = lax.axis_index("tensor")
    tok_grp = arrivals.shape[0]
    feat_part = arrivals.shape[1]
    units = deal.shape[1]
    unit_rows = tok_grp // units
    slot_count = groups * MOST
    width = unit_rows * feat_part
    dest_row = deal[0]
    target = dest_row // units
    position = dest_row % units
    unit_index = jnp.arange(units, dtype=jnp.int32)
    earlier = unit_index[:, None] > unit_index[None, :]
    same_target = target[:, None] == target[None, :]
    rank = jnp.sum(jnp.logical_and(earlier, same_target), axis=1)
    slot = target * MOST + rank
    send_hot = slot[None, :] == jnp.arange(slot_count, dtype=jnp.int32)[:, None]
    filled = jnp.any(send_hot, axis=1)
    slot_pos = jnp.where(filled, jnp.sum(jnp.where(send_hot, position[None, :], 0), axis=1), -1)
    send_matrix = send_hot.astype(jnp.bfloat16)
    packed = jnp.dot(
        send_matrix, arrivals.reshape(units, width), preferred_element_type=jnp.float32
    ).astype(jnp.bfloat16)
    received, recv_pos = (
        lax.all_to_all(
            packed.reshape(groups, MOST, width), "dp", split_axis=0, concat_axis=0, tiled=True
        ),
        lax.all_to_all(
            slot_pos.reshape(groups, MOST), "dp", split_axis=0, concat_axis=0, tiled=True
        ),
    )
    recv_matrix = (recv_pos.reshape(-1)[None, :] == unit_index[:, None]).astype(jnp.bfloat16)
    grouped = jnp.dot(
        recv_matrix, received.reshape(slot_count, width), preferred_element_type=jnp.float32
    ).astype(jnp.bfloat16)
    grouped = grouped.reshape(tok_grp, feat_part)
    full = lax.all_gather(grouped, "tensor", axis=1, tiled=True)
    normed = rms_scale(full, attn_gain).astype(jnp.bfloat16)
    seg_row = seg_ids[0]
    starts = segment_starts(seg_row)
    index = jnp.arange(tok_grp, dtype=jnp.int32)
    cosine, sine = rope_tables(index - starts, HEAD)
    q_heads = w_query.shape[1] // HEAD
    q_raw = jnp.dot(normed, w_query, preferred_element_type=jnp.float32).reshape(
        tok_grp, q_heads, HEAD
    )
    queries = rotate(rms_scale(q_raw, query_gain), cosine, sine).astype(jnp.bfloat16)
    kv_heads = max(1, KVH // shards)
    kv_first = tensor_rank * KVH // shards
    kv_weight = lax.dynamic_slice_in_dim(w_keyval, kv_first * 2 * HEAD, kv_heads * 2 * HEAD, 1)
    kv_raw = jnp.dot(normed, kv_weight, preferred_element_type=jnp.float32).reshape(
        tok_grp, kv_heads, 2, HEAD
    )
    keys = rotate(rms_scale(kv_raw[:, :, 0], key_gain), cosine, sine).astype(jnp.bfloat16)
    values = kv_raw[:, :, 1].astype(jnp.bfloat16)
    stacked = jnp.stack([keys, values], axis=2).reshape(tok_grp, kv_heads * 2 * HEAD)
    cache_cols = 2 * KVH * HEAD // shards
    offset = tensor_rank * cache_cols - kv_first * 2 * HEAD
    own_cache = lax.dynamic_slice_in_dim(stacked, offset, cache_cols, 1)
    pages = own_cache.reshape(tok_grp // PAGE, PAGE, cache_cols)
    kv_pages = jnp.zeros_like(pages).at[page_table[0]].set(pages)
    share = q_heads // kv_heads
    grouped_q = queries.reshape(tok_grp, kv_heads, share, HEAD)
    scale = 1.0 / math.sqrt(HEAD)
    block = min(BLOCK_ROWS, tok_grp)
    outputs = []
    for first in range(0, tok_grp, block):
        last = first + block
        scores = (
            jnp.einsum(
                "ikgd,jkd->kgij",
                grouped_q[first:last],
                keys[:last],
                preferred_element_type=jnp.float32,
            )
            * scale
        )
        query_rows = index[first:last]
        allowed = jnp.logical_and(
            query_rows[:, None] >= index[None, :last],
            starts[first:last][:, None] <= index[None, :last],
        )
        weights = jnp.where(allowed, jnp.exp(scores), 0.0)
        probs = (weights / jnp.sum(weights, axis=-1, keepdims=True)).astype(jnp.bfloat16)
        mixed = jnp.einsum(
            "kgij,jkd->ikgd", probs, values[:last], preferred_element_type=jnp.float32
        )
        outputs.append(mixed.astype(jnp.bfloat16).reshape(block, q_heads * HEAD))
    attended = jnp.concatenate(outputs, axis=0)
    attn_sum = lax.psum(
        jnp.dot(attended, w_out, preferred_element_type=jnp.float32).astype(jnp.bfloat16), "tensor"
    ).astype(jnp.float32)
    middle = (full.astype(jnp.float32) + attn_sum).astype(jnp.bfloat16)
    ffn_in = rms_scale(middle, ffn_gain).astype(jnp.bfloat16)
    gate = jnp.dot(ffn_in, w_gate, preferred_element_type=jnp.float32)
    upper = jnp.dot(ffn_in, w_up, preferred_element_type=jnp.float32)
    hidden = (jax.nn.silu(gate) * upper).astype(jnp.bfloat16)
    ffn_part = lax.psum_scatter(
        jnp.dot(hidden, w_down, preferred_element_type=jnp.float32).astype(jnp.bfloat16),
        "tensor",
        scatter_dimension=1,
        tiled=True,
    ).astype(jnp.float32)
    own_cols = lax.dynamic_slice_in_dim(middle, tensor_rank * feat_part, feat_part, 1)
    combined = (own_cols.astype(jnp.float32) + ffn_part).astype(jnp.bfloat16)
    back = jnp.dot(
        recv_matrix.T, combined.reshape(units, width), preferred_element_type=jnp.float32
    ).astype(jnp.bfloat16)
    returned = lax.all_to_all(
        back.reshape(groups, MOST, width), "dp", split_axis=0, concat_axis=0, tiled=True
    )
    result = jnp.dot(
        send_matrix.T, returned.reshape(slot_count, width), preferred_element_type=jnp.float32
    ).astype(jnp.bfloat16)
    return (result.reshape(tok_grp, feat_part), kv_pages)


def solution(mesh):
    return jax.shard_map(
        on_device,
        mesh=mesh,
        in_specs=(
            P("dp", "tensor"),
            P("dp", None),
            P("dp", None),
            P("dp", None),
            P(),
            P(None, "tensor"),
            P(),
            P(),
            P(),
            P("tensor", None),
            P(),
            P(None, "tensor"),
            P(None, "tensor"),
            P("tensor", None),
        ),
        out_specs=(P("dp", "tensor"), P("dp", None, "tensor")),
        check_vma=False,
    )
```

profile of v0, /device:TPU:65, one launch (start us, length us, event | category | flops | bytes accessed | tf_op | source)
XLA Modules:
  0.0 368.1 jit_solution(12057154090771228152)
XLA Ops:
  7.2 0.8 and_select_fusion.1
  8.0 0.7 fusion.57
  9.0 0.7 select_n.81
  9.8 8.4 %all-to-all-start = ((s32[32,1,2]{2,1,0:T(1,128)}), s32[32,1,2]{2,1,0:T(1,128)S(1)}, u32[]{:S(2)}, u32[]{:S(2)}) async-start(s32[32,1,2]{2,1,0:T(1,128)} %bitcast.5), calls=%async_computation | async-start | bytes 32768 | tf_op jit(solution)/shard_map/all_to_all | solution.py:92
  18.2 1.3 reshape.501
  19.5 1.5 convolution_convert_fusion.1
  21.0 2.5 reshape.502
  23.5 1.7 all-to-all-done
  25.2 6.3 %all-to-all-start.1 = ((bf16[32,2,8192]{2,1,0:T(2,128)(2,1)}), bf16[32,2,8192]{2,1,0:T(2,128)(2,1)}, u32[]{:S(2)}, u32[]{:S(2)}) async-start(bf16[32,2,8192]{2,1,0:T(2,128)(2,1)} %reshape.502), calls=%async_computation.1 | async-start | bytes 2097152 | tf_op jit(solution)/shard_map/all_to_all | solution.py:89
  31.6 0.5 broadcast.308
  32.1 0.7 reduce.8
  32.9 14.9 %all-to-all-done.1 = bf16[32,2,8192]{2,1,0:T(2,128)(2,1)} async-done(((bf16[32,2,8192]{2,1,0:T(2,128)(2,1)}), bf16[32,2,8192]{2,1,0:T(2,128)(2,1)}, u32[]{:S(2)}, u32[]{:S(2)}) %all-to-all-start.1) | async-done | bytes 1048608 | tf_op jit(solution)/shard_map/all_to_all | solution.py:89
  47.8 2.3 reshape.503
  50.1 1.5 convolution_convert_fusion.3
  51.6 1.0 reshape.504
  52.9 0.5 slice.71
  54.1 0.3 reduce-window.9
  54.8 0.5 multiply_cosine_fusion
  55.3 1.0 compare_and_fusion
  56.3 0.5 fusion.10
  56.8 52.7 %all-gather.2.cloned.1.call-done = bf16[1024,2048]{1,0:T(8,128)(2,1)} async-done(((bf16[1024,256]{1,0:T(8,128)(2,1)}), bf16[1024,2048]{1,0:T(8,128)(2,1)}) %all-gather.2.cloned.1.call-update) | async-done | bytes 4194320 | tf_op jit(solution)/shard_map/all_gather | solution.py:101
  109.5 3.2 fusion.3
  113.0 2.6 fusion.19
  115.8 0.6 fusion.34
  116.4 1.6 multiply_reduce_fusion
  118.2 0.8 fusion.11
  119.0 1.1 fusion.7
  120.1 1.3 fusion.21
  121.4 0.7 convolution_convert_fusion.6
  122.2 0.3 copy-done.4
  122.5 3.3 convolution_convert_fusion.5
  125.8 0.3 reduce-scatter.2.cloned.1.call-start
  126.0 116.0 %all-reduce.2.cloned.1.call-done = bf16[1024,2048]{1,0:T(8,128)(2,1)} async-done(((bf16[1024,2048]{1,0:T(8,128)(2,1)}), bf16[1024,2048]{1,0:T(8,128)(2,1)}) %all-reduce.2.cloned.1.call-update) | async-done | bytes 4194320 | tf_op jit(solution)/shard_map/psum | solution.py:154
  242.0 5.6 %fusion = (f32[1024]{0:T(1024)S(1)}, bf16[1024,2048]{1,0:T(8,128)(2,1)S(1)}) fusion(bf16[1024,2048]{1,0:T(8,128)(2,1)} %all-reduce.2.cloned.1.call-done, bf16[1024,2048]{1,0:T(8,128)(2,1)} %all-gather.2.cloned.1.call-done), kind=kLoop, calls=%fused_computation.10 | loop fusion | flops 14679040 | bytes 12587008 | tf_op jit(solution)/shard_map/reduce_sum | solution.py:18
  247.6 1.9 copy-done.2
  249.6 5.1 %fusion.13 = f32[1024,640]{1,0:T(8,128)} fusion(bf16[2048,640]{1,0:T(8,128)(2,1)S(1)} %copy-done.13, bf16[1024,2048]{1,0:T(8,128)(2,1)S(1)} %get-tuple-element.3, f32[2048]{0:T(1024)S(1)} %copy-done.17, f32[1024]{0:T(1024)S(1)} %add_rsqrt_fusion.1), kind=kOutput, calls=%fused_computation.31 | convolution fusion | flops 2692743168 | bytes 9449472 | tf_op jit(solution)/shard_map/dot_general | solution.py:159
  254.6 12.3 %convolution_convert_fusion.4 = bf16[1024,2048]{1,0:T(8,128)(2,1)} fusion(bf16[640,2048]{1,0:T(8,128)(2,1)S(1)} %copy-done, f32[1024,640]{1,0:T(8,128)} %fusion.13, bf16[2048,640]{1,0:T(8,128)(2,1)} %param.26, bf16[1024,2048]{1,0:T(8,128)(2,1)} %copy-done.2, f32[2048]{0:T(1024)S(1)} %copy-done.17, f32[1024]{0:T(1024)S(1)} %add_rsqrt_fusion.1), kind=kOutput, calls=%fused_computation.19 | convolution fusion | flops 5383127040 | bytes 16265216 | tf_op jit(solution)/shard_map/dot_general | solution.py:163
  267.0 59.3 %reduce-scatter.2.cloned.1.call-done = bf16[1024,256]{1,0:T(8,128)(2,1)} async-done(((bf16[1024,2048]{1,0:T(8,128)(2,1)}), bf16[1024,256]{1,0:T(8,128)(2,1)}) %reduce-scatter.2.cloned.1.call-update) | async-done | bytes 524304 | tf_op jit(solution)/shard_map/reduce_scatter | solution.py:162
  326.3 1.3 add_convert_fusion
  327.6 1.0 reshape.514
  328.7 2.5 convolution_convert_fusion
  331.2 2.5 reshape.515
  333.7 6.5 %all-to-all-start.2 = ((bf16[32,2,8192]{2,1,0:T(2,128)(2,1)}), bf16[32,2,8192]{2,1,0:T(2,128)(2,1)}, u32[]{:S(2)}, u32[]{:S(2)}) async-start(bf16[32,2,8192]{2,1,0:T(2,128)(2,1)} %reshape.515), calls=%async_computation.3 | async-start | bytes 2097152 | tf_op jit(solution)/shard_map/all_to_all | solution.py:173
  340.4 0.8 scatter_fusion
  341.2 15.5 %all-to-all-done.2 = bf16[32,2,8192]{2,1,0:T(2,128)(2,1)} async-done(((bf16[32,2,8192]{2,1,0:T(2,128)(2,1)}), bf16[32,2,8192]{2,1,0:T(2,128)(2,1)}, u32[]{:S(2)}, u32[]{:S(2)}) %all-to-all-start.2) | async-done | bytes 1048608 | tf_op jit(solution)/shard_map/all_to_all | solution.py:173
  356.6 2.3 reshape.516
  358.9 1.6 convolution_convert_fusion.2
  360.5 1.0 reshape.517
  (71 shorter events, 1.9 us)
Async XLA Ops:
  7.2 247.5 %copy-start = (bf16[640,2048]{1,0:T(8,128)(2,1)S(1)}, bf16[640,2048]{1,0:T(8,128)(2,1)}, u32[]{:S(2)}) copy-start(bf16[640,2048]{1,0:T(8,128)(2,1)} %param.27) | copy-start | bytes 7864324
  9.8 15.4 %all-to-all-start = ((s32[32,1,2]{2,1,0:T(1,128)}), s32[32,1,2]{2,1,0:T(1,128)S(1)}, u32[]{:S(2)}, u32[]{:S(2)}) async-start(s32[32,1,2]{2,1,0:T(1,128)} %bitcast.5), calls=%async_computation | async-start | bytes 32768 | tf_op jit(solution)/shard_map/all_to_all | solution.py:92
  23.5 29.4 %copy-start.10 = (s32[1,1024]{1,0:T(1,128)S(1)}, s32[1,1024]{1,0:T(1,128)}, u32[]{:S(2)}) copy-start(s32[1,1024]{1,0:T(1,128)} %param.16) | copy-start | bytes 12292
  25.2 22.6 %all-to-all-start.1 = ((bf16[32,2,8192]{2,1,0:T(2,128)(2,1)}), bf16[32,2,8192]{2,1,0:T(2,128)(2,1)}, u32[]{:S(2)}, u32[]{:S(2)}) async-start(bf16[32,2,8192]{2,1,0:T(2,128)(2,1)} %reshape.502), calls=%async_computation.1 | async-start | bytes 2097152 | tf_op jit(solution)/shard_map/all_to_all | solution.py:89
  31.5 78.0 %all-gather.2.cloned.1.call-start = ((), (), s32[]{:S(2)}) async-start(), calls=%async_computation.4 | async-start | bytes 4718592 | tf_op jit(solution)/shard_map/all_gather | solution.py:101
  50.1 62.7 %copy-start.15 = (f32[2048]{0:T(1024)S(1)}, f32[2048]{0:T(1024)}, u32[]{:S(2)}) copy-start(f32[2048]{0:T(1024)} %param.18) | copy-start | bytes 24580
  52.6 189.4 %all-reduce.2.cloned.1.call-start = ((), (), s32[]{:S(2)}) async-start(), calls=%async_computation.5 | async-start | bytes 8388608 | tf_op jit(solution)/shard_map/psum | solution.py:154
  109.5 3.4 copy-start.1
  113.0 2.7 copy-start.11
  113.0 3.4 copy-start.14
  113.0 3.4 copy-start.16
  116.4 2.6 copy-start.6
  116.4 2.6 copy-start.8
  116.4 1.6 copy-start.12
  116.4 1.8 copy-start.5
  121.4 1.0 copy-start.4
  125.8 123.8 %copy-start.17 = (f32[2048]{0:T(1024)S(1)}, f32[2048]{0:T(1024)}, u32[]{:S(2)}) copy-start(f32[2048]{0:T(1024)} %param.24) | copy-start | bytes 24580
  125.8 200.5 %reduce-scatter.2.cloned.1.call-start = ((), (), s32[]{:S(2)}) async-start(), calls=%async_computation.6 | async-start | bytes 4718592 | tf_op jit(solution)/shard_map/reduce_scatter | solution.py:162
  242.0 7.5 %copy-start.13 = (bf16[2048,640]{1,0:T(8,128)(2,1)S(1)}, bf16[2048,640]{1,0:T(8,128)(2,1)}, u32[]{:S(2)}) copy-start(bf16[2048,640]{1,0:T(8,128)(2,1)} %param.25) | copy-start | bytes 7864324
  247.6 1.9 copy-start.2
  267.0 73.3 %copy-start.18 = (s32[1,8]{1,0:T(1,128)S(1)}, s32[1,8]{1,0:T(1,128)}, u32[]{:S(2)}) copy-start(s32[1,8]{1,0:T(1,128)} %param.17) | copy-start | bytes 100
  267.0 73.3 %copy-start.7 = (bf16[1024,1,32]{0,2,1:T(8,128)(2,1)S(1)}, bf16[1024,1,32]{0,2,1:T(8,128)(2,1)}, u32[]{:S(2)}) copy-start(bf16[1024,1,32]{0,2,1:T(8,128)(2,1)} %copy-done.6) | copy-start | bytes 196612
  267.0 73.3 %copy-start.9 = (bf16[1024,1,32]{0,2,1:T(8,128)(2,1)S(1)}, bf16[1024,1,32]{0,2,1:T(8,128)(2,1)}, u32[]{:S(2)}) copy-start(bf16[1024,1,32]{0,2,1:T(8,128)(2,1)} %copy-done.8) | copy-start | bytes 196612
  333.7 22.9 %all-to-all-start.2 = ((bf16[32,2,8192]{2,1,0:T(2,128)(2,1)}), bf16[32,2,8192]{2,1,0:T(2,128)(2,1)}, u32[]{:S(2)}, u32[]{:S(2)}) async-start(bf16[32,2,8192]{2,1,0:T(2,128)(2,1)} %reshape.515), calls=%async_computation.3 | async-start | bytes 2097152 | tf_op jit(solution)/shard_map/all_to_all | solution.py:173
  341.2 20.4 %copy-start.3 = (bf16[8,128,64]{1,2,0:T(8,128)(2,1)}, bf16[8,128,64]{1,2,0:T(8,128)(2,1)S(1)}, u32[]{:S(2)}) copy-start(bf16[8,128,64]{1,2,0:T(8,128)(2,1)S(1)} %scatter_fusion) | copy-start | bytes 393220
Sparse Core Ops, SparseCore 0:
  52.8 56.6 all-gather.1
  125.9 116.0 all-reduce.1
  267.1 59.1 reduce-scatter.1
where the time goes:
time: 369 us; the launch traced here: 368 us
  waiting for transfers between devices  260 us (70%)
  matrix products  35.9 us (10%)
  starting transfers between devices  21.8 us (6%)
  local copies, waits for them, and re-layouts  19.4 us (5%)
  other arithmetic  16.1 us (4%)
  between operations  14.9 us (4%)
    psum x1, waiting for transfers between devices, on_device(): lax.psum(jnp.dot(attended, w_out, preferred_element_type=jnp.float32).ast...  116 us
    reduce_scatter x1, waiting for transfers between devices, on_device(): lax.psum_scatter(jnp.dot(hidden, w_down, preferred_element_type=jnp.float...  59.3 us
    all_gather x1, waiting for transfers between devices, on_device(): full = lax.all_gather(grouped, 'tensor', axis=1, tiled=True)  52.7 us
    all_to_all x1, waiting for transfers between devices, on_device(): lax.all_to_all(back.reshape(groups, MOST, width), 'dp', split_axis=0, con...  15.5 us
    all_to_all x1, waiting for transfers between devices, on_device(): lax.all_to_all(packed.reshape(groups, MOST, width), 'dp', split_axis=0, c...  14.9 us
    dot_general x1, matrix products, on_device(): jnp.dot(hidden, w_down, preferred_element_type=jnp.float32)  12.3 us
    reduce_sum x3, other arithmetic, rms_scale(): mean_sq = jnp.mean(values * values, axis=-1, keepdims=True)  8.85 us
    all_to_all x1, starting transfers between devices, on_device(): lax.all_to_all(slot_pos.reshape(groups, MOST), 'dp', split_axis=0, concat...  8.39 us
  transfers between devices with their start and end apart: 6, of which 6 were waited for; matrix products, arithmetic and copies ran while one was open for 3% of the time, Pallas kernels for 0%

commit v1 on v0

--- a/solution.py
+++ b/solution.py
@@ -98,7 +98,9 @@
         recv_matrix, received.reshape(slot_count, width), preferred_element_type=jnp.float32
     ).astype(jnp.bfloat16)
     grouped = grouped.reshape(tok_grp, feat_part)
-    full = lax.all_gather(grouped, "tensor", axis=1, tiled=True)
+    full = jnp.concatenate(
+        lax.all_to_all(jnp.stack([grouped] * lax.axis_size("tensor")), "tensor", 0, 0), axis=1
+    )
     normed = rms_scale(full, attn_gain).astype(jnp.bfloat16)
     seg_row = seg_ids[0]
     starts = segment_starts(seg_row)

time: 369 us -> 421 us (1.14)
  local copies, waits for them, and re-layouts: 19.4 us -> 40.8 us
  waiting for transfers between devices: 260 us -> 275 us
  starting transfers between devices: 21.8 us -> 31 us
  other arithmetic: 16.1 us -> 24.1 us
    all_to_all x0 -> x1, waiting for transfers between devices: none -> 86.9 us  [on_device(): lax.all_to_all(jnp.stack([grouped] * lax.axis_size('tensor')), 'tensor',...]
    all_gather x1 -> x0, waiting for transfers between devices: 52.7 us -> none  [on_device(): full = lax.all_gather(grouped, 'tensor', axis=1, tiled=True)]
    psum x1, waiting for transfers between devices: 116 us -> 97.1 us  [on_device(): lax.psum(jnp.dot(attended, w_out, preferred_element_type=jnp.float32).ast...]
    all_to_all x0 -> x1, starting transfers between devices: none -> 9.51 us  [on_device(): lax.all_to_all(jnp.stack([grouped] * lax.axis_size('tensor')), 'tensor',...]
    convert_element_type x0 -> x1, local copies, waits for them, and re-layouts: none -> 9.17 us  [on_device(): middle = (full.astype(jnp.float32) + attn_sum).astype(jnp.bfloat16)]
    convert_element_type x0 -> x1, other arithmetic: none -> 6.45 us  [on_device(): middle = (full.astype(jnp.float32) + attn_sum).astype(jnp.bfloat16)]
    all_to_all x0 -> x1, local copies, waits for them, and re-layouts: none -> 6.44 us  [on_device(): lax.all_to_all(jnp.stack([grouped] * lax.axis_size('tensor')), 'tensor',...]
  transfers between devices with their start and end apart: 6 -> 6, of which waited for: 6 -> 6; matrix products, arithmetic and copies ran while one was open for 3% -> 7% of each run, Pallas kernels for 0% -> 0%
where the time goes in v1:
time: 421 us; the launch traced here: 420 us
  waiting for transfers between devices  275 us (65%)
  local copies, waits for them, and re-layouts  40.8 us (10%)
  matrix products  34 us (8%)
  starting transfers between devices  31 us (7%)
  other arithmetic  24.1 us (6%)
  between operations  15.1 us (4%)
    psum x1, waiting for transfers between devices, on_device(): lax.psum(jnp.dot(attended, w_out, preferred_element_type=jnp.float32).ast...  97.1 us
    all_to_all x1, waiting for transfers between devices, on_device(): lax.all_to_all(jnp.stack([grouped] * lax.axis_size('tensor')), 'tensor',...  86.9 us
    reduce_scatter x1, waiting for transfers between devices, on_device(): lax.psum_scatter(jnp.dot(hidden, w_down, preferred_element_type=jnp.float...  59.2 us
    all_to_all x1, waiting for transfers between devices, on_device(): lax.all_to_all(back.reshape(groups, MOST, width), 'dp', split_axis=0, con...  15.5 us
    all_to_all x1, waiting for transfers between devices, on_device(): lax.all_to_all(packed.reshape(groups, MOST, width), 'dp', split_axis=0, c...  14.9 us
    dot_general x1, matrix products, on_device(): jnp.dot(hidden, w_down, preferred_element_type=jnp.float32)  12.3 us
    all_to_all x1, starting transfers between devices, on_device(): lax.all_to_all(jnp.stack([grouped] * lax.axis_size('tensor')), 'tensor',...  9.51 us
    reduce_sum x3, other arithmetic, rms_scale(): mean_sq = jnp.mean(values * values, axis=-1, keepdims=True)  9.31 us
  transfers between devices with their start and end apart: 6, of which 6 were waited for; matrix products, arithmetic and copies ran while one was open for 7% of the time, Pallas kernels for 0%

profile of v1, /device:TPU:65, one launch (start us, length us, event | category | flops | bytes accessed | tf_op | source)
XLA Modules:
  0.0 420.2 jit_solution(12551661456044844505)
XLA Ops:
  7.2 0.8 fusion.47
  9.0 0.7 select_n.81
  9.8 8.4 %all-to-all-start = ((s32[32,1,2]{2,1,0:T(1,128)}), s32[32,1,2]{2,1,0:T(1,128)S(1)}, u32[]{:S(2)}, u32[]{:S(2)}) async-start(s32[32,1,2]{2,1,0:T(1,128)} %bitcast.5), calls=%async_computation | async-start | bytes 32768 | tf_op jit(solution)/shard_map/all_to_all | solution.py:92
  18.2 1.3 reshape.528
  19.5 1.5 convolution_convert_fusion.1
  21.0 2.5 reshape.529
  23.5 1.7 all-to-all-done
  25.2 6.2 %all-to-all-start.1 = ((bf16[32,2,8192]{2,1,0:T(2,128)(2,1)}), bf16[32,2,8192]{2,1,0:T(2,128)(2,1)}, u32[]{:S(2)}, u32[]{:S(2)}) async-start(bf16[32,2,8192]{2,1,0:T(2,128)(2,1)} %reshape.529), calls=%async_computation.1 | async-start | bytes 2097152 | tf_op jit(solution)/shard_map/all_to_all | solution.py:89
  31.9 0.7 reduce.10
  32.7 14.9 %all-to-all-done.1 = bf16[32,2,8192]{2,1,0:T(2,128)(2,1)} async-done(((bf16[32,2,8192]{2,1,0:T(2,128)(2,1)}), bf16[32,2,8192]{2,1,0:T(2,128)(2,1)}, u32[]{:S(2)}, u32[]{:S(2)}) %all-to-all-start.1) | async-done | bytes 1048608 | tf_op jit(solution)/shard_map/all_to_all | solution.py:89
  47.6 2.3 reshape.530
  49.9 2.3 convolution_convert_fusion.3
  52.2 1.3 stack_reshape.2
  53.5 2.2 stack.8
  55.7 9.5 %all-to-all-start.2 = ((bf16[8,1024,256]{2,1,0:T(8,128)(2,1)}), bf16[8,1024,256]{2,1,0:T(8,128)(2,1)}, u32[]{:S(2)}, u32[]{:S(2)}) async-start(bf16[8,1024,256]{2,1,0:T(8,128)(2,1)} %stack.8), calls=%async_computation.2 | async-start | bytes 8388608 | tf_op jit(solution)/shard_map/all_to_all | solution.py:102
  66.9 1.0 copy.47
  67.9 1.1 dynamic-slice_bitcast_fusion
  69.0 1.1 copy.45
  70.8 1.0 compare_and_fusion
  72.3 86.9 %all-to-all-done.2 = bf16[8,1024,256]{2,1,0:T(8,128)(2,1)} async-done(((bf16[8,1024,256]{2,1,0:T(8,128)(2,1)}), bf16[8,1024,256]{2,1,0:T(8,128)(2,1)}, u32[]{:S(2)}, u32[]{:S(2)}) %all-to-all-start.2) | async-done | bytes 4194336 | tf_op jit(solution)/shard_map/all_to_all | solution.py:102
  159.2 6.4 %copy.43 = bf16[8,1024,256]{1,2,0:T(8,128)(2,1)} copy(bf16[8,1024,256]{2,1,0:T(8,128)(2,1)} %all-to-all-done.2) | data formatting | bytes 8388608 | tf_op jit(solution)/shard_map/all_to_all | solution.py:102
  165.7 3.3 multiply_reduce_fusion
  169.1 1.1 multiply_convert_fusion
  170.2 0.7 convolution_bitcast_fusion
  171.2 0.7 multiply_reduce_fusion.1
  172.9 0.8 fusion.7
  173.7 1.1 fusion.3
  174.8 1.3 fusion.13
  176.2 0.7 convolution_convert_fusion.6
  177.2 3.2 convolution_convert_fusion.5
  180.7 6.5 %convert_element_type.166 = f32[8,1024,256]{1,2,0:T(8,128)} convert(bf16[8,1024,256]{1,2,0:T(8,128)(2,1)} %copy.43) | non-fusion elementwise | flops 2097152 | bytes 12582912 | tf_op jit(solution)/shard_map/convert_element_type | solution.py:159
  187.2 9.2 %copy.56 = f32[1024,2048]{1,0:T(8,128)} copy(f32[1024,2048]{0,1:T(8,128)} %bitcast.148) | data formatting | bytes 16777216 | tf_op jit(solution)/shard_map/convert_element_type | solution.py:159
  196.4 97.1 %all-reduce.2.cloned.1.call-done = bf16[1024,2048]{1,0:T(8,128)(2,1)} async-done(((bf16[1024,2048]{1,0:T(8,128)(2,1)}), bf16[1024,2048]{1,0:T(8,128)(2,1)}) %all-reduce.2.cloned.1.call-update) | async-done | bytes 4194320 | tf_op jit(solution)/shard_map/psum | solution.py:156
  293.4 6.0 %fusion = (f32[1024]{0:T(1024)S(1)}, bf16[1024,2048]{1,0:T(8,128)(2,1)S(1)}) fusion(f32[1024,2048]{1,0:T(8,128)} %copy.56, bf16[1024,2048]{1,0:T(8,128)(2,1)} %all-reduce.2.cloned.1.call-done), kind=kLoop, calls=%fused_computation.7 | loop fusion | flops 12581888 | bytes 16781312 | tf_op jit(solution)/shard_map/reduce_sum | solution.py:18
  299.5 1.9 copy-done.2
  301.4 5.1 %fusion.9 = f32[1024,640]{1,0:T(8,128)} fusion(bf16[2048,640]{1,0:T(8,128)(2,1)S(1)} %copy-done.17, bf16[1024,2048]{1,0:T(8,128)(2,1)S(1)} %get-tuple-element.3, f32[2048]{0:T(1024)S(1)} %copy-done.18, f32[1024]{0:T(1024)S(1)} %add_rsqrt_fusion.1), kind=kOutput, calls=%fused_computation.28 | convolution fusion | flops 2692743168 | bytes 9449472 | tf_op jit(solution)/shard_map/dot_general | solution.py:161
  306.5 12.3 %convolution_convert_fusion.4 = bf16[1024,2048]{1,0:T(8,128)(2,1)} fusion(bf16[640,2048]{1,0:T(8,128)(2,1)S(1)} %copy-done, f32[1024,640]{1,0:T(8,128)} %fusion.9, bf16[2048,640]{1,0:T(8,128)(2,1)} %param.26, bf16[1024,2048]{1,0:T(8,128)(2,1)} %copy-done.2, f32[2048]{0:T(1024)S(1)} %copy-done.18, f32[1024]{0:T(1024)S(1)} %add_rsqrt_fusion.1), kind=kOutput, calls=%fused_computation.15 | convolution fusion | flops 5383127040 | bytes 16265216 | tf_op jit(solution)/shard_map/dot_general | solution.py:165
  318.8 59.2 %reduce-scatter.2.cloned.1.call-done = bf16[1024,256]{1,0:T(8,128)(2,1)} async-done(((bf16[1024,2048]{1,0:T(8,128)(2,1)}), bf16[1024,256]{1,0:T(8,128)(2,1)}) %reduce-scatter.2.cloned.1.call-update) | async-done | bytes 524304 | tf_op jit(solution)/shard_map/reduce_scatter | solution.py:164
  378.0 1.3 add_convert_fusion.1
  379.4 1.0 reshape.539
  380.4 2.5 convolution_convert_fusion
  382.9 2.5 reshape.540
  385.4 6.7 %all-to-all-start.3 = ((bf16[32,2,8192]{2,1,0:T(2,128)(2,1)}), bf16[32,2,8192]{2,1,0:T(2,128)(2,1)}, u32[]{:S(2)}, u32[]{:S(2)}) async-start(bf16[32,2,8192]{2,1,0:T(2,128)(2,1)} %reshape.540), calls=%async_computation.4 | async-start | bytes 2097152 | tf_op jit(solution)/shard_map/all_to_all | solution.py:175
  392.3 0.7 scatter_fusion
  393.0 15.5 %all-to-all-done.3 = bf16[32,2,8192]{2,1,0:T(2,128)(2,1)} async-done(((bf16[32,2,8192]{2,1,0:T(2,128)(2,1)}), bf16[32,2,8192]{2,1,0:T(2,128)(2,1)}, u32[]{:S(2)}, u32[]{:S(2)}) %all-to-all-start.3) | async-done | bytes 1048608 | tf_op jit(solution)/shard_map/all_to_all | solution.py:175
  408.5 2.3 reshape.541
  410.8 1.6 convolution_convert_fusion.2
  412.3 1.0 reshape.542
  (81 shorter events, 6.0 us)
Async XLA Ops:
  7.2 299.3 %copy-start = (bf16[640,2048]{1,0:T(8,128)(2,1)S(1)}, bf16[640,2048]{1,0:T(8,128)(2,1)}, u32[]{:S(2)}) copy-start(bf16[640,2048]{1,0:T(8,128)(2,1)} %param.27) | copy-start | bytes 7864324
  9.8 15.4 %all-to-all-start = ((s32[32,1,2]{2,1,0:T(1,128)}), s32[32,1,2]{2,1,0:T(1,128)S(1)}, u32[]{:S(2)}, u32[]{:S(2)}) async-start(s32[32,1,2]{2,1,0:T(1,128)} %bitcast.5), calls=%async_computation | async-start | bytes 32768 | tf_op jit(solution)/shard_map/all_to_all | solution.py:92
  25.2 22.4 %all-to-all-start.1 = ((bf16[32,2,8192]{2,1,0:T(2,128)(2,1)}), bf16[32,2,8192]{2,1,0:T(2,128)(2,1)}, u32[]{:S(2)}, u32[]{:S(2)}) async-start(bf16[32,2,8192]{2,1,0:T(2,128)(2,1)} %reshape.529), calls=%async_computation.1 | async-start | bytes 2097152 | tf_op jit(solution)/shard_map/all_to_all | solution.py:89
  55.7 9.5 %copy-start.13 = (s32[1,1024]{1,0:T(1,128)S(1)}, s32[1,1024]{1,0:T(1,128)}, u32[]{:S(2)}) copy-start(s32[1,1024]{1,0:T(1,128)} %param.16) | copy-start | bytes 12292
  55.7 11.2 %copy-start.14 = (f32[2048]{0:T(1024)S(1)}, f32[2048]{0:T(1024)}, u32[]{:S(2)}) copy-start(f32[2048]{0:T(1024)} %param.18) | copy-start | bytes 24580
  55.7 11.2 %copy-start.5 = (bf16[2048,128]{1,0:T(8,128)(2,1)S(1)}, bf16[2048,128]{1,0:T(8,128)(2,1)}, u32[]{:S(2)}) copy-start(bf16[2048,128]{1,0:T(8,128)(2,1)} %param.19) | copy-start | bytes 1572868
  55.7 103.5 %all-to-all-start.2 = ((bf16[8,1024,256]{2,1,0:T(8,128)(2,1)}), bf16[8,1024,256]{2,1,0:T(8,128)(2,1)}, u32[]{:S(2)}, u32[]{:S(2)}) async-start(bf16[8,1024,256]{2,1,0:T(8,128)(2,1)} %stack.8), calls=%async_computation.2 | async-start | bytes 8388608 | tf_op jit(solution)/shard_map/all_to_all | solution.py:102
  65.2 228.2 %all-reduce.2.cloned.1.call-start = ((), (), s32[]{:S(2)}) async-start(), calls=%async_computation.5 | async-start | bytes 8388608 | tf_op jit(solution)/shard_map/psum | solution.py:156
  165.7 3.4 copy-start.1
  169.1 1.1 copy-start.7
  170.2 1.0 copy-start.6
  170.9 1.1 copy-start.15
  171.0 1.7 copy-start.16
  171.2 1.7 copy-start.8
  172.7 2.1 copy-start.9
  172.7 2.1 copy-start.11
  176.2 1.0 copy-start.4
  180.5 197.6 %reduce-scatter.2.cloned.1.call-start = ((), (), s32[]{:S(2)}) async-start(), calls=%async_computation.6 | async-start | bytes 4718592 | tf_op jit(solution)/shard_map/reduce_scatter | solution.py:164
  196.4 105.0 %copy-start.18 = (f32[2048]{0:T(1024)S(1)}, f32[2048]{0:T(1024)}, u32[]{:S(2)}) copy-start(f32[2048]{0:T(1024)} %param.24) | copy-start | bytes 24580
  293.4 7.9 %copy-start.17 = (bf16[2048,640]{1,0:T(8,128)(2,1)S(1)}, bf16[2048,640]{1,0:T(8,128)(2,1)}, u32[]{:S(2)}) copy-start(bf16[2048,640]{1,0:T(8,128)(2,1)} %param.25) | copy-start | bytes 7864324
  299.4 1.9 copy-start.2
  318.8 73.3 %copy-start.19 = (s32[1,8]{1,0:T(1,128)S(1)}, s32[1,8]{1,0:T(1,128)}, u32[]{:S(2)}) copy-start(s32[1,8]{1,0:T(1,128)} %param.17) | copy-start | bytes 100
  318.8 73.3 %copy-start.10 = (bf16[1024,1,32]{0,2,1:T(8,128)(2,1)S(1)}, bf16[1024,1,32]{0,2,1:T(8,128)(2,1)}, u32[]{:S(2)}) copy-start(bf16[1024,1,32]{0,2,1:T(8,128)(2,1)} %copy-done.9) | copy-start | bytes 196612
  318.8 73.3 %copy-start.12 = (bf16[1024,1,32]{0,2,1:T(8,128)(2,1)S(1)}, bf16[1024,1,32]{0,2,1:T(8,128)(2,1)}, u32[]{:S(2)}) copy-start(bf16[1024,1,32]{0,2,1:T(8,128)(2,1)} %copy-done.11) | copy-start | bytes 196612
  385.4 23.0 %all-to-all-start.3 = ((bf16[32,2,8192]{2,1,0:T(2,128)(2,1)}), bf16[32,2,8192]{2,1,0:T(2,128)(2,1)}, u32[]{:S(2)}, u32[]{:S(2)}) async-start(bf16[32,2,8192]{2,1,0:T(2,128)(2,1)} %reshape.540), calls=%async_computation.4 | async-start | bytes 2097152 | tf_op jit(solution)/shard_map/all_to_all | solution.py:175
  393.0 20.4 %copy-start.3 = (bf16[8,128,64]{1,2,0:T(8,128)(2,1)}, bf16[8,128,64]{1,2,0:T(8,128)(2,1)S(1)}, u32[]{:S(2)}) copy-start(bf16[8,128,64]{1,2,0:T(8,128)(2,1)S(1)} %scatter_fusion) | copy-start | bytes 393220
Sparse Core Ops, SparseCore 0:
  180.6 112.7 all-reduce.1
  318.9 59.0 reduce-scatter.1
